TPU v7x, 32 devices: a whole 2x2x4 slice. The times are simulated.
32 devices in a mesh: grid: 4 (over z), mode: 8 (over y, x, core).
Axes of the slice: x: 2, y: 2, z: 4, core: 2. Of those that a mesh axis runs over, the one named last changes fastest.
Arguments:
- modes_field: bfloat16 [512, 192, 1024], P('mode', 'grid'), may hold values from -6 to 6
- chaos_basis: bfloat16 [512, 512], replicated, may hold values from -0.25 to 0.25
- node_weights: float32 [512], replicated, may hold values from 0.5 to 2
- node_points: float32 [512, 16], replicated, may hold values from -4 to 4
- kl_fields: float32 [16, 192, 1024], P(None, 'grid'), may hold values from -0.6 to 0.6
- velocity: float32 [2, 192, 1024], P(None, 'grid'), may hold values from -4 to 4
Outputs:
- tendency: bfloat16 [512, 192, 1024], P('mode', 'grid')
All inputs are finite; a program needn't handle non-finite values.
Results may differ from a plain program's by a relative error of at most 0.0053.
Values may be sent and summed in bfloat16 or wider, within the bound.
No kernel may reach another device: no remote copies, remote signals or barrier semaphores. Data moves between devices by JAX's collectives and lax.ppermute only.
A program may use at most 128 MiB of HBM per device.

v0:
```python
import jax
import jax.numpy as jnp
from jax import lax
from jax.sharding import PartitionSpec as P


def extended(cells, sides, width):
    for axis, dim in sides:
        count = lax.axis_size(axis)
        ends = count - 1
        head = lax.slice_in_dim(cells, 0, width, axis=dim)
        tail = lax.slice_in_dim(cells, cells.shape[dim] - width, cells.shape[dim], axis=dim)
        cells = jnp.concatenate(
            [
                lax.ppermute(tail, axis, [(i, (i + 1) % count) for i in range(ends)]),
                cells,
                lax.ppermute(head, axis, [((i + 1) % count, i) for i in range(ends)]),
            ],
            axis=dim,
        )
    return cells


def node_terms(padded_field, kl_piece, node_points, velocity_piece, node_weights):
    field_value = padded_field.astype(jnp.float32)
    viscosity = jnp.exp(
        jnp.einsum("qk,krc->qrc", node_points, kl_piece, precision=lax.Precision.HIGHEST)
    )
    center = field_value[:, 1:-1, 1:-1]
    visc_center = viscosity[:, 1:-1, 1:-1]

    def face_flux(near_field, near_visc):
        return 0.5 * (visc_center + near_visc) * (near_field - center)

    north = field_value[:, 2:, 1:-1]
    south = field_value[:, :-2, 1:-1]
    east = field_value[:, 1:-1, 2:]
    west = field_value[:, 1:-1, :-2]
    diffusion = face_flux(north, viscosity[:, 2:, 1:-1]) + face_flux(south, viscosity[:, :-2, 1:-1])
    diffusion = (
        diffusion
        + face_flux(east, viscosity[:, 1:-1, 2:])
        + face_flux(west, viscosity[:, 1:-1, :-2])
    )
    advection = 0.5 * velocity_piece[0] * (north - south) + 0.5 * velocity_piece[1] * (east - west)
    flux = diffusion - advection
    return (node_weights[:, None, None] * flux).astype(jnp.bfloat16)


def local(modes_field, chaos_basis, node_weights, node_points, kl_fields, velocity):
    kl_rimmed = extended(kl_fields, (("grid", 1),), 1)
    kl_rimmed = jnp.pad(kl_rimmed, ((0, 0), (0, 0), (1, 1)))
    result = jnp.einsum(
        "qp,prc->qrc",
        chaos_basis,
        lax.all_to_all(modes_field, "mode", split_axis=2, concat_axis=0, tiled=True),
        preferred_element_type=jnp.float32,
    )
    nodal = result.astype(jnp.bfloat16)
    node_blocks = lax.all_to_all(nodal, "mode", split_axis=0, concat_axis=2, tiled=True)
    rimmed = extended(node_blocks, (("grid", 1),), 1)
    padded_field = jnp.pad(rimmed, ((0, 0), (0, 0), (1, 1)))
    node_share = node_blocks.shape[0]
    first_index = lax.axis_index("mode") * node_share
    point_part = lax.dynamic_slice_in_dim(node_points, first_index, node_share, 0)
    weight_part = lax.dynamic_slice_in_dim(node_weights, first_index, node_share, 0)
    weighted = node_terms(padded_field, kl_rimmed, point_part, velocity, weight_part)
    cell_terms = lax.all_to_all(weighted, "mode", split_axis=2, concat_axis=0, tiled=True)
    tendency = jnp.einsum(
        "qp,qrc->prc", chaos_basis, cell_terms, preferred_element_type=jnp.float32
    )
    tendency = tendency.astype(jnp.bfloat16)
    return lax.all_to_all(tendency, "mode", split_axis=0, concat_axis=2, tiled=True)


def solution(mesh):
    return jax.shard_map(
        local,
        mesh=mesh,
        in_specs=(
            P("mode", "grid", None),
            P(),
            P(),
            P(),
            P(None, "grid", None),
            P(None, "grid", None),
        ),
        out_specs=P("mode", "grid", None),
        check_vma=False,
    )
```

profile of v0, /device:TPU:0, one launch (start us, length us, event | category | flops | bytes accessed | tf_op | source)
XLA Modules:
  0.0 571.1 jit_solution(2297330801579381977)
XLA Ops:
  0.0 0.0 copy-start
  0.0 20.8 %copy.58 = bf16[64,48,1024]{0,1,2:T(8,128)(2,1)} copy(bf16[64,48,1024]{2,1,0:T(8,128)(2,1)} %param.6) | data formatting | bytes 12582912 | tf_op args[0]
  20.8 13.7 %reshape.3 = bf16[8,2,196608]{2,1,0:T(2,128)(2,1)} reshape(bf16[1024,48,64]{2,1,0:T(8,128)(2,1)} %bitcast.48) | data formatting | bytes 12582912
  34.5 77.6 %all_to_all.72 = bf16[8,2,196608]{2,1,0:T(2,128)(2,1)} all-to-all(bf16[8,2,196608]{2,1,0:T(2,128)(2,1)} %reshape.3), channel_id=1, replica_groups=mesh['grid'=4,'mode'=8] {'mode'}, dimensions={0} | all-to-all | bytes 12582912 | tf_op jit(solution)/shard_map/all_to_all | solution.py:56
  112.1 13.3 %reshape.4 = bf16[1024,48,64]{2,1,0:T(8,128)(2,1)} reshape(bf16[8,2,196608]{2,1,0:T(2,128)(2,1)} %all_to_all.72) | data formatting | bytes 12582912
  125.4 14.1 %copy.59 = bf16[64,48,8,128]{3,0,2,1:T(8,128)(2,1)} copy(bf16[64,48,8,128]{0,1,3,2:T(8,128)(2,1)} %bitcast.45) | data formatting | bytes 12582912 | tf_op jit(solution)/shard_map/all_to_all | solution.py:56
  139.5 0.0 copy-done
  139.5 6.4 %convolution_convert_fusion = bf16[512,48,128]{2,0,1:T(8,128)(2,1)S(1)} fusion(bf16[512,48,128]{2,0,1:T(8,128)(2,1)} %bitcast.54, bf16[512,512]{1,0:T(8,128)(2,1)S(1)} %copy-done), kind=kOutput, calls=%fused_computation.40 | convolution fusion | flops 3224371200 | bytes 13107200 | tf_op jit(solution)/shard_map/qp,prc->qrc/dot_general | solution.py:53
  145.9 6.8 %copy.60 = bf16[512,48,128]{2,1,0:T(8,128)(2,1)} copy(bf16[512,48,128]{2,0,1:T(8,128)(2,1)S(1)} %convolution_convert_fusion) | data formatting | bytes 12582912 | tf_op jit(solution)/shard_map/convert_element_type | solution.py:59
  152.7 0.0 copy-start.2
  152.7 5.1 all-to-all-start.1
  157.8 3.7 copy.55
  161.5 0.0 copy-start.1
  161.5 1.7 copy-done.1
  163.2 4.3 collective-permute-start
  167.5 1.3 collective-permute-start.1
  168.8 0.8 dynamic_slice.6
  169.5 0.0 copy-done.2
  169.6 59.6 %all-to-all-done.1 = bf16[512,48,128]{2,1,0:T(8,128)(2,1)} async-done(((bf16[512,48,128]{2,1,0:T(8,128)(2,1)}), bf16[512,48,128]{2,1,0:T(8,128)(2,1)}, u32[]{:S(2)}, u32[]{:S(2)}) %all-to-all-start.1) | async-done | bytes 6291488 | tf_op jit(solution)/shard_map/all_to_all | solution.py:60
  229.2 9.5 %copy.75 = bf16[8,64,48,128]{3,0,1,2:T(8,128)(2,1)} copy(bf16[8,64,48,128]{3,2,1,0:T(8,128)(2,1)} %bitcast.5) | data formatting | bytes 12582912 | tf_op jit(solution)/shard_map/all_to_all | solution.py:60
  238.7 10.3 %all_to_all.59 = bf16[64,48,1024]{2,0,1:T(8,128)(2,1)} reshape(bf16[64,48,8,128]{3,2,0,1:T(8,128)(2,1)} %bitcast.51) | data formatting | bytes 12582912 | tf_op jit(solution)/shard_map/all_to_all | solution.py:60
  249.0 0.0 slice-start
  249.0 1.1 fusion.39
  250.2 4.4 collective-permute-start.2
  254.6 0.0 slice-start.1
  254.6 1.6 collective-permute-start.3
  256.2 0.0 collective-permute-done
  256.2 0.0 collective-permute-done.1
  256.2 16.3 %convolution_exponential_fusion = f32[64,50,1026]{2,0,1:T(8,128)} fusion(f32[16,1,1024]{2,0,1:T(8,128)S(1)} %collective-permute-done.1, f32[16,48,1024]{2,0,1:T(8,128)} %copy-done.1, f32[16,1,1024]{2,0,1:T(8,128)S(1)} %collective-permute-done, f32[512,16]{0,1:T(8,128)} %param.9, s32[]{:T(128)S(6)} %select_n.4), kind=kOutput, calls=%fused_computation.2 | convolution fusion | flops 636940800 | bytes 16417796 | tf_op jit(solution)/shard_map/qk,krc->qrc/dot_general | solution.py:27
  272.5 0.0 collective-permute-done.2
  272.5 0.0 collective-permute-done.3
  272.5 0.0 slice-done
  272.5 0.0 slice-done.1
  272.5 7.0 %fusion.20 = f32[64,50,1026]{2,0,1:T(8,128)} fusion(bf16[64,1,1024]{2,0,1:T(8,128)(2,1)S(1)} %collective-permute-done.3, bf16[64,48,1024]{2,0,1:T(8,128)(2,1)S(1)} %bitcast.50, bf16[64,1,1024]{2,0,1:T(8,128)(2,1)S(1)} %collective-permute-done.2), kind=kLoop, calls=%fused_computation.27 | loop fusion | flops 39398400 | bytes 19686400 | tf_op jit(solution)/shard_map/convert_element_type | solution.py:25
  279.5 60.8 %fusion.6 = bf16[64,48,1024]{2,0,1:T(8,128)(2,1)} fusion(f32[64,50,1026]{2,0,1:T(8,128)} %convolution_exponential_fusion, f32[64,50,1026]{2,0,1:T(8,128)} %fusion.20, f32[48,1024]{1,0:T(8,128)S(1)} %get-tuple-element.10, f32[48,1024]{1,0:T(8,128)S(1)} %get-tuple-element.9, f32[64]{0:T(128)S(1)} %dynamic_slice.6), kind=kLoop, calls=%fused_computation.10 | loop fusion | flops 84934656 | bytes 132514048 | tf_op jit(solution)/shard_map/convert_element_type | solution.py:47
  340.4 15.7 %copy.62 = bf16[64,48,1024]{0,1,2:T(8,128)(2,1)} copy(bf16[64,48,1024]{2,0,1:T(8,128)(2,1)} %fusion.6) | data formatting | bytes 12582912 | tf_op jit(solution)/shard_map/convert_element_type | solution.py:47
  356.1 13.7 %reshape.5 = bf16[8,2,196608]{2,1,0:T(2,128)(2,1)} reshape(bf16[1024,48,64]{2,1,0:T(8,128)(2,1)} %bitcast.46) | data formatting | bytes 12582912
  369.8 76.9 %all_to_all.73 = bf16[8,2,196608]{2,1,0:T(2,128)(2,1)} all-to-all(bf16[8,2,196608]{2,1,0:T(2,128)(2,1)} %reshape.5), channel_id=1, replica_groups=mesh['grid'=4,'mode'=8] {'mode'}, dimensions={0} | all-to-all | bytes 12582912 | tf_op jit(solution)/shard_map/all_to_all | solution.py:68
  446.7 13.3 %reshape.6 = bf16[1024,48,64]{2,1,0:T(8,128)(2,1)} reshape(bf16[8,2,196608]{2,1,0:T(2,128)(2,1)} %all_to_all.73) | data formatting | bytes 12582912
  460.0 14.1 %copy.70 = bf16[8,64,48,128]{3,1,0,2:T(8,128)(2,1)} copy(bf16[8,64,48,128]{1,2,3,0:T(8,128)(2,1)} %bitcast.47) | data formatting | bytes 12582912 | tf_op jit(solution)/shard_map/all_to_all | solution.py:68
  474.1 8.2 %convert_bitcast_fusion = bf16[512,48,128]{0,2,1:T(8,128)(2,1)} fusion(bf16[512,48,128]{2,0,1:T(8,128)(2,1)} %bitcast.53, bf16[512,512]{1,0:T(8,128)(2,1)S(1)} %copy-done), kind=kOutput, calls=%fused_computation.30 | convolution fusion | flops 3224371200 | bytes 13107200 | tf_op jit(solution)/shard_map/qp,qrc->prc/dot_general | solution.py:69
  482.4 9.0 %copy.66 = bf16[512,48,128]{2,1,0:T(8,128)(2,1)} copy(bf16[512,48,128]{0,2,1:T(8,128)(2,1)} %convert_bitcast_fusion) | data formatting | bytes 12582912 | tf_op jit(solution)/shard_map/convert_element_type | solution.py:72
  491.3 75.2 %all_to_all.74 = bf16[512,48,128]{2,1,0:T(8,128)(2,1)S(1)} all-to-all(bf16[512,48,128]{2,1,0:T(8,128)(2,1)} %copy.66), channel_id=1, replica_groups=mesh['grid'=4,'mode'=8] {'mode'}, dimensions={0} | all-to-all | bytes 12582912 | tf_op jit(solution)/shard_map/all_to_all | solution.py:73
  566.5 4.5 copy.74
  (3 shorter events, 0.0 us)
Async XLA Ops:
  0.0 139.5 %copy-start = (bf16[512,512]{1,0:T(8,128)(2,1)S(1)}, bf16[512,512]{1,0:T(8,128)(2,1)}, u32[]{:S(2)}) copy-start(bf16[512,512]{1,0:T(8,128)(2,1)} %param.7) | copy-start | bytes 1572868
  152.7 16.8 %copy-start.2 = (f32[2,48,1024]{2,1,0:T(8,128)S(1)}, f32[2,48,1024]{2,1,0:T(8,128)}, u32[]{:S(2)}) copy-start(f32[2,48,1024]{2,1,0:T(8,128)} %param.11) | copy-start | bytes 1179652
  152.7 76.5 %all-to-all-start.1 = ((bf16[512,48,128]{2,1,0:T(8,128)(2,1)}), bf16[512,48,128]{2,1,0:T(8,128)(2,1)}, u32[]{:S(2)}, u32[]{:S(2)}) async-start(bf16[512,48,128]{2,1,0:T(8,128)(2,1)} %copy.60), calls=%async_computation.1 | async-start | bytes 12582912 | tf_op jit(solution)/shard_map/all_to_all | solution.py:60
  161.5 1.7 copy-start.1
  163.2 93.0 %collective-permute-start = (f32[16,1,1024]{2,0,1:T(8,128)S(1)}, f32[16,1,1024]{2,0,1:T(8,128)S(1)}, u32[]{:S(2)}, u32[]{:S(2)}) collective-permute-start(f32[16,1,1024]{2,0,1:T(8,128)S(1)} %get-tuple-element.7), channel_id=1, source_target_pairs={{0,8},{8,16},{16,24},{1,9},{9,17},{17,25},{2,10},{10,18},{18,26},{... | collective-permute-start | bytes 196616 | tf_op jit(solution)/shard_map/ppermute | solution.py:15
  167.5 88.8 %collective-permute-start.1 = (f32[16,1,1024]{2,0,1:T(8,128)S(1)}, f32[16,1,1024]{2,0,1:T(8,128)S(1)}, u32[]{:S(2)}, u32[]{:S(2)}) collective-permute-start(f32[16,1,1024]{2,0,1:T(8,128)S(1)} %get-tuple-element.8), channel_id=1, source_target_pairs={{8,0},{16,8},{24,16},{9,1},{17,9},{25,17},{10,2},{18,10},{26,18},{... | collective-permute-start | bytes 196616 | tf_op jit(solution)/shard_map/ppermute | solution.py:17
  249.0 23.5 %slice-start = ((s8[6291456]{0:T(1024)(128)(4,1)}), s8[4194304]{0:T(1024)(128)(4,1)S(1)}, s32[]{:S(2)}) async-start(s8[6291456]{0:T(1024)(128)(4,1)} %bitcast.49), calls=%async_computation.4 | async-start | bytes 8388608
  250.2 22.3 %collective-permute-start.2 = (bf16[64,1,1024]{2,0,1:T(8,128)(2,1)S(1)}, bf16[64,1,1024]{2,0,1:T(8,128)(2,1)S(1)}, u32[]{:S(2)}, u32[]{:S(2)}) collective-permute-start(bf16[64,1,1024]{2,0,1:T(8,128)(2,1)S(1)} %get-tuple-element.5), channel_id=1, source_target_pairs={{0,8},{8,16},{16,24},{1,9},{9,17},{17,25},{2,10},{10,18},{18,26},{... | collective-permute-start | bytes 393224 | tf_op jit(solution)/shard_map/ppermute | solution.py:15
  254.6 18.0 %slice-start.1 = ((s8[6291456]{0:T(1024)(128)(4,1)}), s8[2097152]{0:T(1024)(128)(4,1)S(1)}, s32[]{:S(2)}) async-start(s8[6291456]{0:T(1024)(128)(4,1)} %bitcast.49), calls=%async_computation.5 | async-start | bytes 4194304
  254.6 17.9 %collective-permute-start.3 = (bf16[64,1,1024]{2,0,1:T(8,128)(2,1)S(1)}, bf16[64,1,1024]{2,0,1:T(8,128)(2,1)S(1)}, u32[]{:S(2)}, u32[]{:S(2)}) collective-permute-start(bf16[64,1,1024]{2,0,1:T(8,128)(2,1)S(1)} %get-tuple-element.6), channel_id=1, source_target_pairs={{8,0},{16,8},{24,16},{9,1},{17,9},{25,17},{10,2},{18,10},{26,18},{... | collective-permute-start | bytes 393224 | tf_op jit(solution)/shard_map/ppermute | solution.py:17
where the time goes:
time: 574 us; the launch traced here: 571 us
  blocking collectives  230 us (40%)
  local copies, waits for them, and re-layouts  166 us (29%)
  other arithmetic  67.9 us (12%)
  waiting for transfers between devices  59.6 us (10%)
  matrix products  30.9 us (5%)
  starting transfers between devices  16.7 us (3%)
    unnamed x16, local copies, waits for them, and re-layouts  80.3 us
    all_to_all x1, blocking collectives, local(): lax.all_to_all(modes_field, 'mode', split_axis=2, concat_axis=0, tiled=True)  77.6 us
    all_to_all x1, blocking collectives, local(): lax.all_to_all(weighted, 'mode', split_axis=2, concat_axis=0, tiled=True)  76.9 us
    all_to_all x1, blocking collectives, local(): lax.all_to_all(tendency, 'mode', split_axis=0, concat_axis=2, tiled=True)  75.2 us
    convert_element_type x1, other arithmetic, node_terms(): return (node_weights[:, None, None] * flux).astype(jnp.bfloat16)  60.8 us
    all_to_all x1, waiting for transfers between devices, local(): lax.all_to_all(nodal, 'mode', split_axis=0, concat_axis=2, tiled=True)  59.6 us
    all_to_all x2, local copies, waits for them, and re-layouts, local(): lax.all_to_all(nodal, 'mode', split_axis=0, concat_axis=2, tiled=True)  19.8 us
    dot_general x1, matrix products, node_terms(): jnp.einsum('qk,krc->qrc', node_points, kl_piece, precision=lax.Precision....  16.3 us
  transfers between devices with their start and end apart: 5, of which 1 were waited for; matrix products, arithmetic and copies ran while one was open for 6% of the time, Pallas kernels for 0%

commit v1 on v0

--- a/solution.py
+++ b/solution.py
@@ -1,7 +1,24 @@
+import functools
 import jax
 import jax.numpy as jnp
 from jax import lax
 from jax.sharding import PartitionSpec as P
+
+
+def _guide_yards(message, comm_axis):
+    carry_in = jnp.concatenate(
+        lax.all_to_all(
+            jnp.stack(jnp.split(message, lax.axis_size(comm_axis), axis=2)),
+            axis_name=comm_axis,
+            split_axis=0,
+            concat_axis=0,
+        ),
+        axis=0,
+    )
+    return carry_in
+
+
+_move_hubs = functools.partial(_guide_yards, comm_axis="mode")
 
 
 def extended(cells, sides, width):
@@ -51,10 +68,7 @@
     kl_rimmed = extended(kl_fields, (("grid", 1),), 1)
     kl_rimmed = jnp.pad(kl_rimmed, ((0, 0), (0, 0), (1, 1)))
     result = jnp.einsum(
-        "qp,prc->qrc",
-        chaos_basis,
-        lax.all_to_all(modes_field, "mode", split_axis=2, concat_axis=0, tiled=True),
-        preferred_element_type=jnp.float32,
+        "qp,prc->qrc", chaos_basis, _move_hubs(modes_field), preferred_element_type=jnp.float32
     )
     nodal = result.astype(jnp.bfloat16)
     node_blocks = lax.all_to_all(nodal, "mode", split_axis=0, concat_axis=2, tiled=True)

time: 574 us -> 522 us (0.909)
  local copies, waits for them, and re-layouts: 166 us -> 116 us
    unnamed x16 -> x20, local copies, waits for them, and re-layouts: 80.3 us -> 41.2 us
    all_to_all x1 -> x0, local copies, waits for them, and re-layouts: 14.1 us -> none  [local(): lax.all_to_all(modes_field, 'mode', split_axis=2, concat_axis=0, tiled=True)]
where the time goes in v1:
time: 522 us; the launch traced here: 519 us
  blocking collectives  229 us (44%)
  local copies, waits for them, and re-layouts  116 us (22%)
  other arithmetic  67.9 us (13%)
  waiting for transfers between devices  60.5 us (12%)
  matrix products  30.5 us (6%)
  starting transfers between devices  14.8 us (3%)
    all_to_all x1, blocking collectives, local(): lax.all_to_all(weighted, 'mode', split_axis=2, concat_axis=0, tiled=True)  76.9 us
    all_to_all x1, blocking collectives, _guide_yards(): lax.all_to_all(jnp.stack(jnp.split(message, lax.axis_size(comm_axis), axi...  76.5 us
    all_to_all x1, blocking collectives, local(): lax.all_to_all(tendency, 'mode', split_axis=0, concat_axis=2, tiled=True)  75.2 us
    convert_element_type x1, other arithmetic, node_terms(): return (node_weights[:, None, None] * flux).astype(jnp.bfloat16)  60.8 us
    all_to_all x1, waiting for transfers between devices, local(): lax.all_to_all(nodal, 'mode', split_axis=0, concat_axis=2, tiled=True)  60.5 us
    unnamed x20, local copies, waits for them, and re-layouts  41.2 us
    all_to_all x2, local copies, waits for them, and re-layouts, local(): lax.all_to_all(nodal, 'mode', split_axis=0, concat_axis=2, tiled=True)  19.8 us
    dot_general x1, matrix products, node_terms(): jnp.einsum('qk,krc->qrc', node_points, kl_piece, precision=lax.Precision....  16.3 us
  transfers between devices with their start and end apart: 5, of which 1 were waited for; matrix products, arithmetic and copies ran while one was open for 6% of the time, Pallas kernels for 0%

profile of v1, /device:TPU:0, one launch (start us, length us, event | category | flops | bytes accessed | tf_op | source)
XLA Modules:
  0.0 518.9 jit_solution(8017692092937050127)
XLA Ops:
  0.0 0.0 copy-start
  0.0 1.2 bitcast_dynamic-update-slice_fusion.7
  1.2 1.2 bitcast_dynamic-update-slice_fusion.6
  2.5 1.2 bitcast_dynamic-update-slice_fusion.5
  3.7 1.2 bitcast_dynamic-update-slice_fusion.4
  5.0 1.2 bitcast_dynamic-update-slice_fusion.3
  6.2 1.2 bitcast_dynamic-update-slice_fusion.2
  7.5 1.2 bitcast_dynamic-update-slice_fusion.1
  8.7 1.2 bitcast_dynamic-update-slice_fusion
  9.9 76.5 %all_to_all.59 = bf16[8,64,48,128]{3,2,1,0:T(8,128)(2,1)S(1)} all-to-all(bf16[8,64,48,128]{3,2,1,0:T(8,128)(2,1)S(1)} %bitcast_dynamic-update-slice_fusion), channel_id=1, replica_groups=mesh['grid'=4,'mode'=8] {'mode'}, dimensions={0} | all-to-all | bytes 12582912 | tf_op jit(solution)/shard_map/all_to_all | solution.py:10
  86.4 0.0 copy-done
  86.5 6.0 %convert_bitcast_fusion.1 = bf16[512,48,128]{0,2,1:T(8,128)(2,1)} fusion(bf16[512,48,128]{2,1,0:T(8,128)(2,1)S(1)} %bitcast.62, bf16[512,512]{1,0:T(8,128)(2,1)S(1)} %copy-done), kind=kOutput, calls=%fused_computation.32 | convolution fusion | flops 3224371200 | bytes 13107200 | tf_op jit(solution)/shard_map/qp,prc->qrc/dot_general | solution.py:70
  92.5 9.1 %copy.47 = bf16[512,48,128]{2,1,0:T(8,128)(2,1)} copy(bf16[512,48,128]{0,2,1:T(8,128)(2,1)} %convert_bitcast_fusion.1) | data formatting | bytes 12582912 | tf_op jit(solution)/shard_map/convert_element_type | solution.py:73
  101.6 4.8 all-to-all-start.1
  106.3 0.0 copy-start.2
  106.4 3.8 copy.43
  110.1 0.0 copy-start.1
  110.1 1.7 copy-done.1
  111.8 3.5 collective-permute-start
  115.3 1.3 collective-permute-start.1
  116.6 0.8 dynamic_slice.6
  117.4 0.0 copy-done.2
  117.4 60.5 %all-to-all-done.1 = bf16[512,48,128]{2,1,0:T(8,128)(2,1)} async-done(((bf16[512,48,128]{2,1,0:T(8,128)(2,1)}), bf16[512,48,128]{2,1,0:T(8,128)(2,1)}, u32[]{:S(2)}, u32[]{:S(2)}) %all-to-all-start.1) | async-done | bytes 6291488 | tf_op jit(solution)/shard_map/all_to_all | solution.py:74
  177.9 9.5 %copy.48 = bf16[64,48,8,128]{3,2,0,1:T(8,128)(2,1)} copy(bf16[64,48,8,128]{3,1,0,2:T(8,128)(2,1)} %bitcast.13) | data formatting | bytes 12582912 | tf_op jit(solution)/shard_map/all_to_all | solution.py:74
  187.5 10.3 %all_to_all.46 = bf16[64,48,1024]{2,0,1:T(8,128)(2,1)} reshape(bf16[64,48,8,128]{3,2,0,1:T(8,128)(2,1)} %copy.48) | data formatting | bytes 12582912 | tf_op jit(solution)/shard_map/all_to_all | solution.py:74
  197.8 1.0 fusion.43
  198.8 3.5 collective-permute-start.2
  202.3 0.0 slice-start
  202.3 0.0 slice-start.1
  202.3 1.7 collective-permute-start.3
  204.0 0.0 collective-permute-done
  204.0 0.0 collective-permute-done.1
  204.0 16.3 %convolution_exponential_fusion = f32[64,50,1026]{2,0,1:T(8,128)} fusion(f32[16,1,1024]{2,0,1:T(8,128)S(1)} %collective-permute-done.1, f32[16,48,1024]{2,0,1:T(8,128)} %copy-done.1, f32[16,1,1024]{2,0,1:T(8,128)S(1)} %collective-permute-done, f32[512,16]{0,1:T(8,128)} %param.9, s32[]{:T(128)S(6)} %select_n.4), kind=kOutput, calls=%fused_computation.2 | convolution fusion | flops 636940800 | bytes 16417796 | tf_op jit(solution)/shard_map/qk,krc->qrc/dot_general | solution.py:44
  220.3 0.0 collective-permute-done.2
  220.4 0.0 collective-permute-done.3
  220.4 0.0 slice-done
  220.4 0.0 slice-done.1
  220.4 7.0 %fusion.20 = f32[64,50,1026]{2,0,1:T(8,128)} fusion(bf16[64,1,1024]{2,0,1:T(8,128)(2,1)S(1)} %collective-permute-done.3, bf16[64,48,1024]{2,0,1:T(8,128)(2,1)S(1)} %bitcast.59, bf16[64,1,1024]{2,0,1:T(8,128)(2,1)S(1)} %collective-permute-done.2), kind=kLoop, calls=%fused_computation.27 | loop fusion | flops 39398400 | bytes 19686400 | tf_op jit(solution)/shard_map/convert_element_type | solution.py:42
  227.4 60.8 %fusion.6 = bf16[64,48,1024]{2,0,1:T(8,128)(2,1)} fusion(f32[64,50,1026]{2,0,1:T(8,128)} %convolution_exponential_fusion, f32[64,50,1026]{2,0,1:T(8,128)} %fusion.20, f32[48,1024]{1,0:T(8,128)S(1)} %get-tuple-element.10, f32[48,1024]{1,0:T(8,128)S(1)} %get-tuple-element.9, f32[64]{0:T(128)S(1)} %dynamic_slice.6), kind=kLoop, calls=%fused_computation.10 | loop fusion | flops 84934656 | bytes 132514048 | tf_op jit(solution)/shard_map/convert_element_type | solution.py:64
  288.2 15.7 %copy.49 = bf16[64,48,1024]{0,1,2:T(8,128)(2,1)} copy(bf16[64,48,1024]{2,0,1:T(8,128)(2,1)} %fusion.6) | data formatting | bytes 12582912 | tf_op jit(solution)/shard_map/convert_element_type | solution.py:64
  303.9 13.7 %reshape.7 = bf16[8,2,196608]{2,1,0:T(2,128)(2,1)} reshape(bf16[1024,48,64]{2,1,0:T(8,128)(2,1)} %bitcast.56) | data formatting | bytes 12582912
  317.7 76.9 %all_to_all.60 = bf16[8,2,196608]{2,1,0:T(2,128)(2,1)} all-to-all(bf16[8,2,196608]{2,1,0:T(2,128)(2,1)} %reshape.7), channel_id=1, replica_groups=mesh['grid'=4,'mode'=8] {'mode'}, dimensions={0} | all-to-all | bytes 12582912 | tf_op jit(solution)/shard_map/all_to_all | solution.py:82
  394.5 13.3 %reshape.8 = bf16[1024,48,64]{2,1,0:T(8,128)(2,1)} reshape(bf16[8,2,196608]{2,1,0:T(2,128)(2,1)} %all_to_all.60) | data formatting | bytes 12582912
  407.9 14.1 %copy.57 = bf16[8,64,48,128]{3,1,0,2:T(8,128)(2,1)} copy(bf16[8,64,48,128]{1,2,3,0:T(8,128)(2,1)} %bitcast.57) | data formatting | bytes 12582912 | tf_op jit(solution)/shard_map/all_to_all | solution.py:82
  422.0 8.2 %convert_bitcast_fusion = bf16[512,48,128]{0,2,1:T(8,128)(2,1)} fusion(bf16[512,48,128]{2,0,1:T(8,128)(2,1)} %bitcast.61, bf16[512,512]{1,0:T(8,128)(2,1)S(1)} %copy-done), kind=kOutput, calls=%fused_computation.31 | convolution fusion | flops 3224371200 | bytes 13107200 | tf_op jit(solution)/shard_map/qp,qrc->prc/dot_general | solution.py:83
  430.2 9.0 %copy.53 = bf16[512,48,128]{2,1,0:T(8,128)(2,1)} copy(bf16[512,48,128]{0,2,1:T(8,128)(2,1)} %convert_bitcast_fusion) | data formatting | bytes 12582912 | tf_op jit(solution)/shard_map/convert_element_type | solution.py:86
  439.2 75.2 %all_to_all.61 = bf16[512,48,128]{2,1,0:T(8,128)(2,1)S(1)} all-to-all(bf16[512,48,128]{2,1,0:T(8,128)(2,1)} %copy.53), channel_id=1, replica_groups=mesh['grid'=4,'mode'=8] {'mode'}, dimensions={0} | all-to-all | bytes 12582912 | tf_op jit(solution)/shard_map/all_to_all | solution.py:87
  514.4 4.5 copy.64
  (3 shorter events, 0.0 us)
Async XLA Ops:
  0.0 86.4 %copy-start = (bf16[512,512]{1,0:T(8,128)(2,1)S(1)}, bf16[512,512]{1,0:T(8,128)(2,1)}, u32[]{:S(2)}) copy-start(bf16[512,512]{1,0:T(8,128)(2,1)} %param.7) | copy-start | bytes 1572868
  101.6 76.4 %all-to-all-start.1 = ((bf16[512,48,128]{2,1,0:T(8,128)(2,1)}), bf16[512,48,128]{2,1,0:T(8,128)(2,1)}, u32[]{:S(2)}, u32[]{:S(2)}) async-start(bf16[512,48,128]{2,1,0:T(8,128)(2,1)} %copy.47), calls=%async_computation.1 | async-start | bytes 12582912 | tf_op jit(solution)/shard_map/all_to_all | solution.py:74
  106.3 11.1 %copy-start.2 = (f32[2,48,1024]{2,1,0:T(8,128)S(1)}, f32[2,48,1024]{2,1,0:T(8,128)}, u32[]{:S(2)}) copy-start(f32[2,48,1024]{2,1,0:T(8,128)} %param.11) | copy-start | bytes 1179652
  110.1 1.7 copy-start.1
  111.8 92.2 %collective-permute-start = (f32[16,1,1024]{2,0,1:T(8,128)S(1)}, f32[16,1,1024]{2,0,1:T(8,128)S(1)}, u32[]{:S(2)}, u32[]{:S(2)}) collective-permute-start(f32[16,1,1024]{2,0,1:T(8,128)S(1)} %get-tuple-element.7), channel_id=1, source_target_pairs={{0,8},{8,16},{16,24},{1,9},{9,17},{17,25},{2,10},{10,18},{18,26},{... | collective-permute-start | bytes 196616 | tf_op jit(solution)/shard_map/ppermute | solution.py:32
  115.3 88.7 %collective-permute-start.1 = (f32[16,1,1024]{2,0,1:T(8,128)S(1)}, f32[16,1,1024]{2,0,1:T(8,128)S(1)}, u32[]{:S(2)}, u32[]{:S(2)}) collective-permute-start(f32[16,1,1024]{2,0,1:T(8,128)S(1)} %get-tuple-element.8), channel_id=1, source_target_pairs={{8,0},{16,8},{24,16},{9,1},{17,9},{25,17},{10,2},{18,10},{26,18},{... | collective-permute-start | bytes 196616 | tf_op jit(solution)/shard_map/ppermute | solution.py:34
  198.8 21.6 %collective-permute-start.2 = (bf16[64,1,1024]{2,0,1:T(8,128)(2,1)S(1)}, bf16[64,1,1024]{2,0,1:T(8,128)(2,1)S(1)}, u32[]{:S(2)}, u32[]{:S(2)}) collective-permute-start(bf16[64,1,1024]{2,0,1:T(8,128)(2,1)S(1)} %get-tuple-element.5), channel_id=1, source_target_pairs={{0,8},{8,16},{16,24},{1,9},{9,17},{17,25},{2,10},{10,18},{18,26},{... | collective-permute-start | bytes 393224 | tf_op jit(solution)/shard_map/ppermute | solution.py:32
  202.3 18.1 %slice-start = ((s8[6291456]{0:T(1024)(128)(4,1)}), s8[4194304]{0:T(1024)(128)(4,1)S(1)}, s32[]{:S(2)}) async-start(s8[6291456]{0:T(1024)(128)(4,1)} %bitcast.58), calls=%async_computation.4 | async-start | bytes 8388608
  202.3 18.1 %slice-start.1 = ((s8[6291456]{0:T(1024)(128)(4,1)}), s8[2097152]{0:T(1024)(128)(4,1)S(1)}, s32[]{:S(2)}) async-start(s8[6291456]{0:T(1024)(128)(4,1)} %bitcast.58), calls=%async_computation.5 | async-start | bytes 4194304
  202.3 18.1 %collective-permute-start.3 = (bf16[64,1,1024]{2,0,1:T(8,128)(2,1)S(1)}, bf16[64,1,1024]{2,0,1:T(8,128)(2,1)S(1)}, u32[]{:S(2)}, u32[]{:S(2)}) collective-permute-start(bf16[64,1,1024]{2,0,1:T(8,128)(2,1)S(1)} %get-tuple-element.6), channel_id=1, source_target_pairs={{8,0},{16,8},{24,16},{9,1},{17,9},{25,17},{10,2},{18,10},{26,18},{... | collective-permute-start | bytes 393224 | tf_op jit(solution)/shard_map/ppermute | solution.py:34
